TPU v7x, 32 devices: a whole 2x2x4 slice. The times are simulated.
32 devices in a mesh: row: 4 (over y, core), col: 8 (over z, x).
Axes of the slice: x: 2, y: 2, z: 4, core: 2. Of those that a mesh axis runs over, the one named last changes fastest.
Arguments:
- bands: float32 [2, 12, 32, 1024], P(None, None, 'row', 'col'), may hold values from -500 to 500
- directions: float32 [2, 12, 32, 1024], P(None, None, 'row', 'col'), may hold values from -500 to 500
- materials: int32 [32, 1024], P('row', 'col'), may hold values from 0 to 7
- permittivity: float32 [8], replicated, may hold values from 1 to 12
- wavevector: int32 [2], replicated, may hold values from 0 to 15
Outputs:
- basis: float32 [2, 36, 32, 1024], P(None, None, 'row', 'col')
- reduced: float32 [2, 36, 36], replicated
All inputs are finite; a program needn't handle non-finite values.
Results may differ from a plain program's by a relative error of at most 0.00018.
Values sent between devices are 32-bit elements; how exact they have to be, the bound alone decides.
No kernel may reach another device: no remote copies, remote signals or barrier semaphores. Data moves between devices by JAX's collectives and lax.ppermute only.
A program may use at most 64 MiB of HBM per device.

v0:
```python
import math
import jax
import jax.numpy as jnp
from jax import lax
from jax.sharding import PartitionSpec as P

KDEN = 16
NS_STEPS = 5


def with_halo(cells, sides, width):
    for axis, dim in sides:
        count = lax.axis_size(axis)
        head = lax.slice_in_dim(cells, 0, width, axis=dim)
        tail = lax.slice_in_dim(cells, cells.shape[dim] - width, cells.shape[dim], axis=dim)
        cells = jnp.concatenate(
            [
                lax.ppermute(tail, axis, [(i, (i + 1) % count) for i in range(count)]),
                cells,
                lax.ppermute(head, axis, [((i + 1) % count, i) for i in range(count)]),
            ],
            axis=dim,
        )
    return cells


def rotate(values, phase_angle):
    cosine = jnp.cos(phase_angle)
    sine_part = jnp.sin(phase_angle)
    return jnp.stack(
        [values[0] * cosine - values[1] * sine_part, values[0] * sine_part + values[1] * cosine]
    )


def bloch_rims(padded, edges, rim_layers):
    low_row, high_row, low_col, high_col = edges
    padded = padded.at[:, :, :rim_layers].set(rotate(padded[:, :, :rim_layers], low_row))
    padded = padded.at[:, :, -rim_layers:].set(rotate(padded[:, :, -rim_layers:], high_row))
    padded = padded.at[:, :, :, :rim_layers].set(rotate(padded[:, :, :, :rim_layers], low_col))
    padded = padded.at[:, :, :, -rim_layers:].set(rotate(padded[:, :, :, -rim_layers:], high_col))
    return padded


def stencil(padded, stiff_pad):
    centre = stiff_pad[1:-1, 1:-1]
    upward = 0.5 * (centre + stiff_pad[:-2, 1:-1])
    downward = 0.5 * (centre + stiff_pad[2:, 1:-1])
    leftward = 0.5 * (centre + stiff_pad[1:-1, :-2])
    rightward = 0.5 * (centre + stiff_pad[1:-1, 2:])
    diagonal = upward + downward + leftward + rightward
    inner_cells = padded[:, :, 1:-1, 1:-1]
    neighbours = (
        upward * padded[:, :, :-2, 1:-1]
        + downward * padded[:, :, 2:, 1:-1]
        + leftward * padded[:, :, 1:-1, :-2]
        + rightward * padded[:, :, 1:-1, 2:]
    )
    return (diagonal * inner_cells - neighbours, diagonal)


def complex_gram(first_block, second_block):
    highest = lax.Precision.HIGHEST
    first_flat = first_block.reshape(first_block.shape[0], first_block.shape[1], -1)
    second_flat = second_block.reshape(second_block.shape[0], second_block.shape[1], -1)
    real_part = jnp.einsum("pjc,pkc->jk", first_flat, second_flat, precision=highest)
    imag_part = jnp.einsum(
        "jc,kc->jk", first_flat[0], second_flat[1], precision=highest
    ) - jnp.einsum("jc,kc->jk", first_flat[1], second_flat[0], precision=highest)
    return (real_part, imag_part)


def inverse_root(gram_real, gram_imag):
    highest = lax.Precision.HIGHEST
    order_size = gram_real.shape[0]
    upper_half = jnp.concatenate([gram_real, -gram_imag], axis=1)
    lower_half = jnp.concatenate([gram_imag, gram_real], axis=1)
    embedded = jnp.concatenate([upper_half, lower_half], axis=0)
    magnitude = jnp.sqrt(jnp.sum(embedded * embedded))
    identity = jnp.eye(2 * order_size, dtype=embedded.dtype)

    def newton(turn_index, carried):
        current, inverse = carried
        factor = 1.5 * identity - 0.5 * jnp.dot(inverse, current, precision=highest)
        return (
            jnp.dot(current, factor, precision=highest),
            jnp.dot(factor, inverse, precision=highest),
        )

    current, inverse = lax.fori_loop(0, NS_STEPS, newton, (embedded / magnitude, identity))
    root_full = inverse / jnp.sqrt(magnitude)
    return (root_full[:order_size, :order_size], root_full[order_size:, :order_size])


def reduce_matrix(root_real, root_imag, ham_real, ham_imag):
    highest = lax.Precision.HIGHEST
    prod_real = jnp.dot(ham_real, root_real, precision=highest) - jnp.dot(
        ham_imag, root_imag, precision=highest
    )
    prod_imag = jnp.dot(ham_real, root_imag, precision=highest) + jnp.dot(
        ham_imag, root_real, precision=highest
    )
    red_real = jnp.dot(root_real.T, prod_real, precision=highest) + jnp.dot(
        root_imag.T, prod_imag, precision=highest
    )
    red_imag = jnp.dot(root_real.T, prod_imag, precision=highest) - jnp.dot(
        root_imag.T, prod_real, precision=highest
    )
    return jnp.stack([red_real, red_imag])


def rotate_basis(raw_basis, root_real, root_imag, scale_factor):
    highest = lax.Precision.HIGHEST
    basis_real = jnp.einsum("jrc,jk->krc", raw_basis[0], root_real, precision=highest) - jnp.einsum(
        "jrc,jk->krc", raw_basis[1], root_imag, precision=highest
    )
    basis_imag = jnp.einsum("jrc,jk->krc", raw_basis[0], root_imag, precision=highest) + jnp.einsum(
        "jrc,jk->krc", raw_basis[1], root_real, precision=highest
    )
    return scale_factor * jnp.stack([basis_real, basis_imag])


def project_mixing(mixing, matrix):
    highest = lax.Precision.HIGHEST
    return jnp.dot(mixing.T, jnp.dot(matrix, mixing, precision=highest), precision=highest)


def body(bands, directions, materials, permittivity, wavevector):
    band_count = bands.shape[1]
    height = bands.shape[2]
    breadth = bands.shape[3]
    levels = jnp.arange(permittivity.shape[0], dtype=jnp.int32)
    stiffness = jnp.sum(
        jnp.where(
            materials[None] == levels[:, None, None], (1.0 / permittivity)[:, None, None], 0.0
        ),
        axis=0,
    )
    angle_row = 2.0 * math.pi * wavevector[0].astype(jnp.float32) / KDEN
    angle_col = 2.0 * math.pi * wavevector[1].astype(jnp.float32) / KDEN
    row_index = lax.axis_index("row")
    col_index = lax.axis_index("col")
    edges = (
        jnp.where(row_index == 0, -angle_row, 0.0),
        jnp.where(row_index == lax.axis_size("row") - 1, angle_row, 0.0),
        jnp.where(col_index == 0, -angle_col, 0.0),
        jnp.where(col_index == lax.axis_size("col") - 1, angle_col, 0.0),
    )
    packed = jnp.concatenate(
        [bands.reshape(2 * band_count, height, breadth), stiffness[None]], axis=0
    )
    padded = with_halo(packed, (("row", 1), ("col", 2)), 1)
    stiff_cycle = padded[-1]
    band_pad = bloch_rims(padded[:-1].reshape(2, band_count, height + 2, breadth + 2), edges, 1)
    applied_cycle, diagonal_cycle = stencil(band_pad, stiff_cycle)
    scaled_cycle = jnp.concatenate([applied_cycle / diagonal_cycle, bands / diagonal_cycle], axis=1)
    stacked = jnp.concatenate([scaled_cycle, directions], axis=1)
    columns_now = stacked.shape[1]
    field_pad = with_halo(
        stacked.reshape(2 * columns_now, height, breadth), (("row", 1), ("col", 2)), 1
    )
    field_pad = bloch_rims(field_pad.reshape(2, columns_now, height + 2, breadth + 2), edges, 1)
    extra_applied = stencil(field_pad, stiff_cycle)[0]
    scaled_image = scaled_cycle[:, :band_count]
    scaled_bands = scaled_cycle[:, band_count:]
    extra = jnp.concatenate([scaled_image, scaled_bands, directions], axis=1)
    extended = jnp.concatenate([bands, extra], axis=1)
    extended_applied = jnp.concatenate([applied_cycle, extra_applied], axis=1)
    local_gram = complex_gram(extended, extended)
    local_ham = complex_gram(extended, extended_applied)
    gram_whole, gram_imag_whole, ham_whole, ham_imag_whole = lax.psum(
        (local_gram[0], local_gram[1], local_ham[0], local_ham[1]), ("row", "col")
    )
    quotient = jnp.diagonal(ham_whole)[:band_count] / jnp.diagonal(gram_whole)[:band_count]
    identity = jnp.eye(band_count, dtype=jnp.float32)
    zeros_block = jnp.zeros((band_count, band_count), jnp.float32)
    mixing = jnp.concatenate(
        [
            jnp.concatenate([identity, zeros_block, zeros_block], axis=1),
            jnp.concatenate([zeros_block, identity, zeros_block], axis=1),
            jnp.concatenate([zeros_block, -jnp.diag(quotient), zeros_block], axis=1),
            jnp.concatenate([zeros_block, zeros_block, identity], axis=1),
        ],
        axis=0,
    )
    gram_real = project_mixing(mixing, gram_whole)
    gram_imag = project_mixing(mixing, gram_imag_whole)
    ham_real = project_mixing(mixing, ham_whole)
    ham_imag = project_mixing(mixing, ham_imag_whole)
    precond = scaled_image - quotient[None, :, None, None] * scaled_bands
    raw_basis = jnp.concatenate([bands, precond, directions], axis=1)
    root_real, root_imag = inverse_root(gram_real, gram_imag)
    scale_factor = math.sqrt(height * breadth * lax.axis_size("row") * lax.axis_size("col"))
    basis = rotate_basis(raw_basis, root_real, root_imag, scale_factor)
    reduced = reduce_matrix(root_real, root_imag, ham_real, ham_imag)
    return (basis, reduced)


def solution(mesh):
    placed = (P(None, None, "row", "col"), P(None, None, "row", "col"), P("row", "col"), P(), P())
    return jax.shard_map(
        body,
        mesh=mesh,
        in_specs=placed,
        out_specs=(P(None, None, "row", "col"), P()),
        check_vma=False,
    )
```

profile of v0, /device:TPU:0, one launch (start us, length us, event | category | flops | bytes accessed | tf_op | source)
XLA Modules:
  0.0 113.8 jit_solution(13991296870753142769)
XLA Ops:
  0.6 1.0 copy.206
  1.6 0.7 broadcast_divide_fusion.4
  2.3 0.8 select_reduce_fusion
  3.1 0.5 collective-permute-start
  3.6 2.0 %collective-permute-start.1 = (f32[25,1,128]{2,0,1:T(8,128)S(1)}, f32[25,1,128]{2,0,1:T(8,128)S(1)}, u32[]{:S(2)}, u32[]{:S(2)}) collective-permute-start(f32[25,1,128]{2,0,1:T(8,128)S(1)} %get-tuple-element.209), channel_id=1, source_target_pairs={{8,0},{16,8},{24,16},{0,24},{9,1},{17,9},{25,17},{1,25},{10,2},{18... | collective-permute-start | bytes 38408 | tf_op jit(solution)/shard_map/ppermute | solution.py:20
  5.6 1.3 %fusion.70 = (s32[1]{0:T(128)}, s32[1]{0:T(128)}) fusion(s32[2]{0:T(128)} %param.27), kind=kLoop, calls=%fused_computation.163 | loop fusion | bytes 16 | tf_op jit(solution)/shard_map/slice | solution.py:139
  7.9 2.3 %collective-permute-start.2 = (f32[25,10,1]{2,0,1:T(8,128)S(1)}, f32[25,10,1]{2,0,1:T(8,128)S(1)}, u32[]{:S(2)}, u32[]{:S(2)}) collective-permute-start(f32[25,10,1]{2,0,1:T(8,128)S(1)} %get-tuple-element.206), channel_id=1, source_target_pairs={{0,1},{1,2},{2,3},{3,4},{4,5},{5,6},{6,7},{7,0},{8,9},{9,10},{10,1... | collective-permute-start | bytes 3008 | tf_op jit(solution)/shard_map/ppermute | solution.py:18
  10.2 3.1 %collective-permute-start.3 = (f32[25,10,1]{2,0,1:T(8,128)S(1)}, f32[25,10,1]{2,0,1:T(8,128)S(1)}, u32[]{:S(2)}, u32[]{:S(2)}) collective-permute-start(f32[25,10,1]{2,0,1:T(8,128)S(1)} %get-tuple-element.207), channel_id=1, source_target_pairs={{1,0},{2,1},{3,2},{4,3},{5,4},{6,5},{7,6},{0,7},{9,8},{10,9},{11,1... | collective-permute-start | bytes 3008 | tf_op jit(solution)/shard_map/ppermute | solution.py:20
  14.4 1.3 %copy.212 = f32[2,12,8,128]{1,3,2,0:T(8,128)} copy(f32[2,12,8,128]{3,2,1,0:T(8,128)S(1)} %copy-done.6) | data formatting | bytes 196608 | tf_op args[0]
  15.7 2.6 %collective-permute-done.2 = f32[25,10,1]{2,0,1:T(8,128)S(1)} collective-permute-done((f32[25,10,1]{2,0,1:T(8,128)S(1)}, f32[25,10,1]{2,0,1:T(8,128)S(1)}, u32[]{:S(2)}, u32[]{:S(2)}) %collective-permute-start.2) | collective-permute-done | bytes 1032 | tf_op jit(solution)/shard_map/ppermute | solution.py:18
  18.3 2.1 %collective-permute-done.3 = f32[25,10,1]{2,0,1:T(8,128)S(1)} collective-permute-done((f32[25,10,1]{2,0,1:T(8,128)S(1)}, f32[25,10,1]{2,0,1:T(8,128)S(1)}, u32[]{:S(2)}, u32[]{:S(2)}) %collective-permute-start.3) | collective-permute-done | bytes 1032 | tf_op jit(solution)/shard_map/ppermute | solution.py:20
  20.6 0.5 copy.210
  21.6 2.8 %broadcast_divide_fusion.1 = (f32[2,12,8,128]{1,3,2,0:T(8,128)S(1)}, f32[2,12,8,128]{1,3,2,0:T(8,128)}, f32[2,12,8,128]{1,3,2,0:T(8,128)S(1)}) fusion(f32[8,128]{1,0:T(8,128)S(1)} %get-tuple-element.181, f32[2,12,10,130]{1,3,2,0:T(8,128)S(1)} %scatter.31, f32[8,128]{1,0:T(8,128)S(1)} %get-tuple-element.185, f32[8,128]{1,0:T(8,128)S(1)} %get-tuple-element.184, ...), kind=kLoop, calls=%fused_computation.62 | loop fusion | flops 270336 | bytes 905216 | tf_op jit(solution)/shard_map/div | solution.py:155
  24.4 0.3 copy.214
  24.7 0.3 copy.215
  25.4 1.7 %collective-permute-start.5 = (f32[72,1,128]{2,1,0:T(1,128)S(1)}, f32[72,1,128]{2,1,0:T(1,128)S(1)}, u32[]{:S(2)}, u32[]{:S(2)}) collective-permute-start(f32[72,1,128]{2,1,0:T(1,128)S(1)} %get-tuple-element.205), channel_id=1, source_target_pairs={{8,0},{16,8},{24,16},{0,24},{9,1},{17,9},{25,17},{1,25},{10,2},{18... | collective-permute-start | bytes 110600 | tf_op jit(solution)/shard_map/ppermute | solution.py:20
  27.2 0.6 fusion.47
  27.8 1.0 collective-permute-done.4
  28.9 1.0 fusion.67
  30.0 1.3 %copy.216 = f32[72,10,1]{0,2,1:T(1,128)S(1)} copy(f32[72,10,1]{2,1,0:T(8,128)} %get-tuple-element.202) | data formatting | bytes 5760 | tf_op jit(solution)/shard_map/slice | solution.py:15
  31.8 4.5 %collective-permute-start.7 = (f32[72,10,1]{0,2,1:T(1,128)S(1)}, f32[72,10,1]{0,2,1:T(1,128)S(1)}, u32[]{:S(2)}, u32[]{:S(2)}) collective-permute-start(f32[72,10,1]{0,2,1:T(1,128)S(1)} %copy.217), channel_id=1, source_target_pairs={{1,0},{2,1},{3,2},{4,3},{5,4},{6,5},{7,6},{0,7},{9,8},{10,9},{11,1... | collective-permute-start | bytes 8648 | tf_op jit(solution)/shard_map/ppermute | solution.py:20
  36.2 1.4 %copy.213 = f32[2,12,8,128]{1,3,2,0:T(8,128)} copy(f32[2,12,8,128]{3,2,1,0:T(8,128)S(1)} %copy-done.5) | data formatting | bytes 196608 | tf_op args[1]
  37.6 0.3 copy.218
  37.9 1.1 copy.219
  39.0 3.0 %pad_maximum_fusion = f32[72,10,130]{2,1,0:T(8,128)} fusion(f32[72,10,1]{2,1,0:T(8,128)} %copy.219, f32[72,1,128]{2,1,0:T(1,128)S(1)} %collective-permute-done.5, f32[72,8,128]{2,1,0:T(8,128)S(1)} %bitcast.123, f32[72,1,128]{2,1,0:T(1,128)S(1)} %collective-permute-done.4, f32[72,10,1]{2,1,0:T(8,128)S(1)} %copy.218), kind=kLoop, calls=%fused_computation.7 | loop fusion | flops 374400 | bytes 748800 | tf_op jit(solution)/shard_map/concatenate | solution.py:16
  42.0 1.8 %copy.223 = f32[2,36,10,130]{1,3,2,0:T(8,128)S(1)} copy(f32[2,36,10,130]{3,2,1,0:T(8,128)} %bitcast.119) | data formatting | bytes 748800 | tf_op jit(solution)/shard_map/reshape | solution.py:161
  44.3 1.8 %fusion.10 = f32[2,36,8,128]{1,3,2,0:T(8,128)S(1)} fusion(f32[2,36,10,130]{1,3,2,0:T(8,128)S(1)} %scatter.39, f32[8,128]{1,0:T(8,128)} %copy-done.8, f32[8,128]{1,0:T(8,128)} %copy-done.7, f32[8,128]{1,0:T(8,128)S(1)} %get-tuple-element.183, f32[8,128]{1,0:T(8,128)S(1)} %get-tuple-element.182, f32[8,128]{1,0:T(8,128)S(1)} %get-tuple-element.181), kind=kLoop, calls=%fused_computation.28 | loop fusion | flops 663552 | bytes 1789952 | tf_op jit(solution)/shard_map/sub | solution.py:58
  46.2 1.1 %pad_maximum_fusion.1 = (f32[2,48,8,128]{1,3,2,0:T(8,128)S(1)}, f32[2,48,8,128]{1,3,2,0:T(8,128)S(1)}) fusion(f32[2,12,8,128]{1,3,2,0:T(8,128)S(1)} %copy-done.3, f32[2,12,8,128]{1,3,2,0:T(8,128)S(1)} %get-tuple-element.210, f32[2,12,8,128]{1,3,2,0:T(8,128)S(1)} %get-tuple-element.179, f32[2,12,8,128]{1,3,2,0:T(8,128)S(1)} %copy-done, ...), kind=kLoop, calls=%fused_computation.44 | loop fusion | flops 393216 | bytes 1572864 | tf_op jit(solution)/shard_map/concatenate | solution.py:166
  47.3 1.1 convolution_bitcast_fusion.2
  48.5 1.0 convolution_bitcast_fusion.4
  49.5 1.1 fusion.5
  50.6 1.0 fusion.6
  51.6 1.8 %convolution_bitcast_fusion.5 = f32[48,48]{1,0:T(8,128)S(1)} fusion(f32[2,48,1024]{1,2,0:T(8,128)S(1)} %bitcast.117), kind=kOutput, calls=%fused_computation.18 | convolution fusion | flops 56623104 | bytes 402432 | tf_op jit(solution)/shard_map/pjc,pkc->jk/dot_general | solution.py:65
  53.4 1.8 %convolution_bitcast_fusion.6 = f32[48,48]{1,0:T(8,128)S(1)} fusion(f32[2,48,1024]{1,2,0:T(8,128)S(1)} %bitcast.118, f32[2,48,1024]{1,2,0:T(8,128)S(1)} %bitcast.120), kind=kOutput, calls=%fused_computation.19 | convolution fusion | flops 56623104 | bytes 795648 | tf_op jit(solution)/shard_map/pjc,pkc->jk/dot_general | solution.py:65
  55.2 40.8 %all-reduce.2 = (f32[48,48]{1,0:T(8,128)S(1)}, f32[48,48]{1,0:T(8,128)S(1)}, f32[48,48]{1,0:T(8,128)S(1)}, f32[48,48]{1,0:T(8,128)S(1)}) all-reduce(f32[48,48]{1,0:T(8,128)S(1)} %convolution_bitcast_fusion.5, f32[48,48]{1,0:T(8,128)S(1)} %convolution_bitcast_fusion.6, ...), channel_id=1, replica_groups=mesh['row'=4,'col'=8] {'row','col'}, use_global_device_ids=true, to_apply=%region_2.3 | all-reduce | flops 9216 | bytes 73728 | tf_op jit(solution)/shard_map/psum | solution.py:170
  96.1 1.0 gather_fusion
  97.0 1.0 gather_fusion.1
  99.6 0.7 multiply_reduce_fusion
  101.5 3.7 %while.21 = (s32[]{:T(128)}, f32[72,72]{0,1:T(8,128)S(1)}, f32[72,72]{1,0:T(8,128)S(1)}, s32[]{:T(128)}) while((s32[]{:T(128)}, f32[72,72]{0,1:T(8,128)S(1)}, f32[72,72]{1,0:T(8,128)S(1)}, s32[]{:T(128)}) %tuple.94), condition=%wide.region_6.7_spmd.clone, body=%wide.region_5.6_spmd.clone.sunk | while | flops 13457666 | bytes 269621 | solution.py:89
  105.9 1.1 copy-done.1
  107.0 0.3 copy-done.4
  107.3 0.6 pad_maximum_fusion.2
  107.9 0.6 fusion.24
  108.5 0.7 fusion.23
  111.0 0.6 copy.245
  111.7 0.7 fusion.4
  112.3 0.6 fusion.3
  113.0 0.8 copy.244
  (110 shorter events, 10.3 us)
Async XLA Ops:
  0.6 13.7 %copy-start.6 = (f32[2,12,8,128]{3,2,1,0:T(8,128)S(1)}, f32[2,12,8,128]{3,2,1,0:T(8,128)}, u32[]{:S(2)}) copy-start(f32[2,12,8,128]{3,2,1,0:T(8,128)} %param.23) | copy-start | bytes 294916
  3.1 4.7 %collective-permute-start = (f32[25,1,128]{2,0,1:T(8,128)S(1)}, f32[25,1,128]{2,0,1:T(8,128)S(1)}, u32[]{:S(2)}, u32[]{:S(2)}) collective-permute-start(f32[25,1,128]{2,0,1:T(8,128)S(1)} %get-tuple-element.208), channel_id=1, source_target_pairs={{0,8},{8,16},{16,24},{24,0},{1,9},{9,17},{17,25},{25,1},{2,10},{10... | collective-permute-start | bytes 38408 | tf_op jit(solution)/shard_map/ppermute | solution.py:18
  3.6 4.2 %collective-permute-start.1 = (f32[25,1,128]{2,0,1:T(8,128)S(1)}, f32[25,1,128]{2,0,1:T(8,128)S(1)}, u32[]{:S(2)}, u32[]{:S(2)}) collective-permute-start(f32[25,1,128]{2,0,1:T(8,128)S(1)} %get-tuple-element.209), channel_id=1, source_target_pairs={{8,0},{16,8},{24,16},{0,24},{9,1},{17,9},{25,17},{1,25},{10,2},{18... | collective-permute-start | bytes 38408 | tf_op jit(solution)/shard_map/ppermute | solution.py:20
  7.9 10.3 %collective-permute-start.2 = (f32[25,10,1]{2,0,1:T(8,128)S(1)}, f32[25,10,1]{2,0,1:T(8,128)S(1)}, u32[]{:S(2)}, u32[]{:S(2)}) collective-permute-start(f32[25,10,1]{2,0,1:T(8,128)S(1)} %get-tuple-element.206), channel_id=1, source_target_pairs={{0,1},{1,2},{2,3},{3,4},{4,5},{5,6},{6,7},{7,0},{8,9},{9,10},{10,1... | collective-permute-start | bytes 3008 | tf_op jit(solution)/shard_map/ppermute | solution.py:18
  10.2 10.1 %collective-permute-start.3 = (f32[25,10,1]{2,0,1:T(8,128)S(1)}, f32[25,10,1]{2,0,1:T(8,128)S(1)}, u32[]{:S(2)}, u32[]{:S(2)}) collective-permute-start(f32[25,10,1]{2,0,1:T(8,128)S(1)} %get-tuple-element.207), channel_id=1, source_target_pairs={{1,0},{2,1},{3,2},{4,3},{5,4},{6,5},{7,6},{0,7},{9,8},{10,9},{11,1... | collective-permute-start | bytes 3008 | tf_op jit(solution)/shard_map/ppermute | solution.py:20
  21.5 2.9 %copy-start.7 = (f32[8,128]{1,0:T(8,128)}, f32[8,128]{1,0:T(8,128)S(1)}, u32[]{:S(2)}) copy-start(f32[8,128]{1,0:T(8,128)S(1)} %get-tuple-element.184) | copy-start | bytes 12292
  21.5 2.9 %copy-start.8 = (f32[8,128]{1,0:T(8,128)}, f32[8,128]{1,0:T(8,128)S(1)}, u32[]{:S(2)}) copy-start(f32[8,128]{1,0:T(8,128)S(1)} %get-tuple-element.185) | copy-start | bytes 12292
  24.4 0.9 copy-start.5
  25.4 3.4 %collective-permute-start.4 = (f32[72,1,128]{2,1,0:T(1,128)S(1)}, f32[72,1,128]{2,1,0:T(1,128)S(1)}, u32[]{:S(2)}, u32[]{:S(2)}) collective-permute-start(f32[72,1,128]{2,1,0:T(1,128)S(1)} %get-tuple-element.204), channel_id=1, source_target_pairs={{0,8},{8,16},{16,24},{24,0},{1,9},{9,17},{17,25},{25,1},{2,10},{10... | collective-permute-start | bytes 110600 | tf_op jit(solution)/shard_map/ppermute | solution.py:18
  25.4 3.4 %collective-permute-start.5 = (f32[72,1,128]{2,1,0:T(1,128)S(1)}, f32[72,1,128]{2,1,0:T(1,128)S(1)}, u32[]{:S(2)}, u32[]{:S(2)}) collective-permute-start(f32[72,1,128]{2,1,0:T(1,128)S(1)} %get-tuple-element.205), channel_id=1, source_target_pairs={{8,0},{16,8},{24,16},{0,24},{9,1},{17,9},{25,17},{1,25},{10,2},{18... | collective-permute-start | bytes 110600 | tf_op jit(solution)/shard_map/ppermute | solution.py:20
  31.2 6.4 %collective-permute-start.6 = (f32[72,10,1]{0,2,1:T(1,128)S(1)}, f32[72,10,1]{0,2,1:T(1,128)S(1)}, u32[]{:S(2)}, u32[]{:S(2)}) collective-permute-start(f32[72,10,1]{0,2,1:T(1,128)S(1)} %copy.216), channel_id=1, source_target_pairs={{0,1},{1,2},{2,3},{3,4},{4,5},{5,6},{6,7},{7,0},{8,9},{9,10},{10,1... | collective-permute-start | bytes 8648 | tf_op jit(solution)/shard_map/ppermute | solution.py:18
  31.8 6.2 %collective-permute-start.7 = (f32[72,10,1]{0,2,1:T(1,128)S(1)}, f32[72,10,1]{0,2,1:T(1,128)S(1)}, u32[]{:S(2)}, u32[]{:S(2)}) collective-permute-start(f32[72,10,1]{0,2,1:T(1,128)S(1)} %copy.217), channel_id=1, source_target_pairs={{1,0},{2,1},{3,2},{4,3},{5,4},{6,5},{7,6},{0,7},{9,8},{10,9},{11,1... | collective-permute-start | bytes 8648 | tf_op jit(solution)/shard_map/ppermute | solution.py:20
  44.3 1.8 %copy-start = (f32[2,12,8,128]{1,3,2,0:T(8,128)S(1)}, f32[2,12,8,128]{1,3,2,0:T(8,128)}, u32[]{:S(2)}) copy-start(f32[2,12,8,128]{1,3,2,0:T(8,128)} %copy.212) | copy-start | bytes 294916
  44.3 1.8 %copy-start.2 = (f32[2,12,8,128]{1,3,2,0:T(8,128)S(1)}, f32[2,12,8,128]{1,3,2,0:T(8,128)}, u32[]{:S(2)}) copy-start(f32[2,12,8,128]{1,3,2,0:T(8,128)} %get-tuple-element.180) | copy-start | bytes 294916
  44.3 1.9 %copy-start.3 = (f32[2,12,8,128]{1,3,2,0:T(8,128)S(1)}, f32[2,12,8,128]{1,3,2,0:T(8,128)}, u32[]{:S(2)}) copy-start(f32[2,12,8,128]{1,3,2,0:T(8,128)} %copy.213) | copy-start | bytes 294916
  53.4 44.7 %copy-start.9 = (f32[12,12]{1,0:T(8,128)S(1)}, f32[12,12]{1,0:T(8,128)}, u32[]{:S(2)}) copy-start(f32[12,12]{1,0:T(8,128)} %fusion.47) | copy-start | bytes 1732
  105.7 1.2 %copy-start.1 = (f32[2,12,8,128]{1,3,2,0:T(8,128)S(1)}, f32[2,12,8,128]{1,3,2,0:T(8,128)}, u32[]{:S(2)}) copy-start(f32[2,12,8,128]{1,3,2,0:T(8,128)} %copy.212) | copy-start | bytes 294916
  105.7 1.5 %copy-start.4 = (f32[2,12,8,128]{1,3,2,0:T(8,128)S(1)}, f32[2,12,8,128]{1,3,2,0:T(8,128)}, u32[]{:S(2)}) copy-start(f32[2,12,8,128]{1,3,2,0:T(8,128)} %copy.213) | copy-start | bytes 294916
where the time goes:
time: 114 us
  blocking collectives  40.8 us (36%)
  local copies, waits for them, and re-layouts  17.8 us (16%)
  matrix products  17.8 us (16%)
  starting transfers between devices  14.4 us (13%)
  other arithmetic  13.1 us (11%)
  waiting for transfers between devices  5.71 us (5%)
  between operations  3.93 us (3%)
    psum x1, blocking collectives, body(): lax.psum((local_gram[0], local_gram[1], local_ham[0], local_ham[1]), ('ro...  40.8 us
    ppermute x4, starting transfers between devices, with_halo(): lax.ppermute(head, axis, [((i + 1) % count, i) for i in range(count)])  11.3 us
    unnamed x26, local copies, waits for them, and re-layouts  5.86 us
    ppermute x4, waiting for transfers between devices, with_halo(): lax.ppermute(tail, axis, [(i, (i + 1) % count) for i in range(count)])  3.62 us
    dot_general x2, matrix products, complex_gram(): jnp.einsum('pjc,pkc->jk', first_flat, second_flat, precision=highest)  3.6 us
    concatenate x4, other arithmetic, with_halo(): jnp.concatenate([lax.ppermute(tail, axis, [(i, (i + 1) % count) for i in...  3.24 us
    ppermute x4, starting transfers between devices, with_halo(): lax.ppermute(tail, axis, [(i, (i + 1) % count) for i in range(count)])  3.13 us
    div x1, other arithmetic, body(): applied_cycle / diagonal_cycle  2.78 us
  transfers between devices with their start and end apart: 8, of which 3 were waited for; matrix products, arithmetic and copies ran while one was open for 5% of the time, Pallas kernels for 0%

commit v1 on v0

--- a/solution.py
+++ b/solution.py
@@ -3,6 +3,7 @@
 import jax.numpy as jnp
 from jax import lax
 from jax.sharding import PartitionSpec as P
+from jax.lax import psum
 
 KDEN = 16
 NS_STEPS = 5
@@ -167,8 +168,8 @@
     extended_applied = jnp.concatenate([applied_cycle, extra_applied], axis=1)
     local_gram = complex_gram(extended, extended)
     local_ham = complex_gram(extended, extended_applied)
-    gram_whole, gram_imag_whole, ham_whole, ham_imag_whole = lax.psum(
-        (local_gram[0], local_gram[1], local_ham[0], local_ham[1]), ("row", "col")
+    gram_whole, gram_imag_whole, ham_whole, ham_imag_whole = psum(
+        psum((local_gram[0], local_gram[1], local_ham[0], local_ham[1]), "col"), "row"
     )
     quotient = jnp.diagonal(ham_whole)[:band_count] / jnp.diagonal(gram_whole)[:band_count]
     identity = jnp.eye(band_count, dtype=jnp.float32)

time: 114 us -> 124 us (1.088)
  blocking collectives: 40.8 us -> 50 us
    psum x1 -> x2, blocking collectives: 40.8 us -> 50 us  [the longest x1 38.7 us: body(): psum((local_gram[0], local_gram[1], local_ham[0], local_ham[1]), 'col')]
  transfers between devices with their start and end apart: 8 -> 8, of which waited for: 3 -> 3; matrix products, arithmetic and copies ran while one was open for 5% -> 4% of each run, Pallas kernels for 0% -> 0%
where the time goes in v1:
time: 124 us; the launch traced here: 123 us
  blocking collectives  50 us (40%)
  local copies, waits for them, and re-layouts  17.8 us (14%)
  matrix products  17.8 us (14%)
  starting transfers between devices  14.4 us (12%)
  other arithmetic  13.1 us (11%)
  waiting for transfers between devices  5.69 us (5%)
  between operations  3.93 us (3%)
    psum x1, blocking collectives, body(): psum((local_gram[0], local_gram[1], local_ham[0], local_ham[1]), 'col')  38.7 us
    psum x1, blocking collectives, body(): psum(psum((local_gram[0], local_gram[1], local_ham[0], local_ham[1]), 'co...  11.3 us
    ppermute x4, starting transfers between devices, with_halo(): lax.ppermute(head, axis, [((i + 1) % count, i) for i in range(count)])  11.3 us
    unnamed x26, local copies, waits for them, and re-layouts  5.89 us
    ppermute x4, waiting for transfers between devices, with_halo(): lax.ppermute(tail, axis, [(i, (i + 1) % count) for i in range(count)])  3.61 us
    dot_general x2, matrix products, complex_gram(): jnp.einsum('pjc,pkc->jk', first_flat, second_flat, precision=highest)  3.6 us
    concatenate x4, other arithmetic, with_halo(): jnp.concatenate([lax.ppermute(tail, axis, [(i, (i + 1) % count) for i in...  3.24 us
    ppermute x4, starting transfers between devices, with_halo(): lax.ppermute(tail, axis, [(i, (i + 1) % count) for i in range(count)])  3.13 us
  transfers between devices with their start and end apart: 8, of which 3 were waited for; matrix products, arithmetic and copies ran while one was open for 4% of the time, Pallas kernels for 0%

profile of v1, /device:TPU:0, one launch (start us, length us, event | category | flops | bytes accessed | tf_op | source)
XLA Modules:
  0.0 123.0 jit_solution(14664520803353210474)
XLA Ops:
  0.6 1.0 copy.206
  1.6 0.7 broadcast_divide_fusion.4
  2.3 0.8 select_reduce_fusion
  3.1 0.5 collective-permute-start
  3.6 2.0 %collective-permute-start.1 = (f32[25,1,128]{2,0,1:T(8,128)S(1)}, f32[25,1,128]{2,0,1:T(8,128)S(1)}, u32[]{:S(2)}, u32[]{:S(2)}) collective-permute-start(f32[25,1,128]{2,0,1:T(8,128)S(1)} %get-tuple-element.213), channel_id=1, source_target_pairs={{8,0},{16,8},{24,16},{0,24},{9,1},{17,9},{25,17},{1,25},{10,2},{18... | collective-permute-start | bytes 38408 | tf_op jit(solution)/shard_map/ppermute | solution.py:21
  5.6 1.3 %fusion.70 = (s32[1]{0:T(128)}, s32[1]{0:T(128)}) fusion(s32[2]{0:T(128)} %param.27), kind=kLoop, calls=%fused_computation.163 | loop fusion | bytes 16 | tf_op jit(solution)/shard_map/slice | solution.py:140
  7.9 2.3 %collective-permute-start.2 = (f32[25,10,1]{2,0,1:T(8,128)S(1)}, f32[25,10,1]{2,0,1:T(8,128)S(1)}, u32[]{:S(2)}, u32[]{:S(2)}) collective-permute-start(f32[25,10,1]{2,0,1:T(8,128)S(1)} %get-tuple-element.210), channel_id=1, source_target_pairs={{0,1},{1,2},{2,3},{3,4},{4,5},{5,6},{6,7},{7,0},{8,9},{9,10},{10,1... | collective-permute-start | bytes 3008 | tf_op jit(solution)/shard_map/ppermute | solution.py:19
  10.2 3.1 %collective-permute-start.3 = (f32[25,10,1]{2,0,1:T(8,128)S(1)}, f32[25,10,1]{2,0,1:T(8,128)S(1)}, u32[]{:S(2)}, u32[]{:S(2)}) collective-permute-start(f32[25,10,1]{2,0,1:T(8,128)S(1)} %get-tuple-element.211), channel_id=1, source_target_pairs={{1,0},{2,1},{3,2},{4,3},{5,4},{6,5},{7,6},{0,7},{9,8},{10,9},{11,1... | collective-permute-start | bytes 3008 | tf_op jit(solution)/shard_map/ppermute | solution.py:21
  14.4 1.3 %copy.212 = f32[2,12,8,128]{1,3,2,0:T(8,128)} copy(f32[2,12,8,128]{3,2,1,0:T(8,128)S(1)} %copy-done.6) | data formatting | bytes 196608 | tf_op args[0]
  15.7 2.6 %collective-permute-done.2 = f32[25,10,1]{2,0,1:T(8,128)S(1)} collective-permute-done((f32[25,10,1]{2,0,1:T(8,128)S(1)}, f32[25,10,1]{2,0,1:T(8,128)S(1)}, u32[]{:S(2)}, u32[]{:S(2)}) %collective-permute-start.2) | collective-permute-done | bytes 1032 | tf_op jit(solution)/shard_map/ppermute | solution.py:19
  18.3 2.1 %collective-permute-done.3 = f32[25,10,1]{2,0,1:T(8,128)S(1)} collective-permute-done((f32[25,10,1]{2,0,1:T(8,128)S(1)}, f32[25,10,1]{2,0,1:T(8,128)S(1)}, u32[]{:S(2)}, u32[]{:S(2)}) %collective-permute-start.3) | collective-permute-done | bytes 1032 | tf_op jit(solution)/shard_map/ppermute | solution.py:21
  20.6 0.5 copy.210
  21.6 2.8 %broadcast_divide_fusion.1 = (f32[2,12,8,128]{1,3,2,0:T(8,128)S(1)}, f32[2,12,8,128]{1,3,2,0:T(8,128)}, f32[2,12,8,128]{1,3,2,0:T(8,128)S(1)}) fusion(f32[8,128]{1,0:T(8,128)S(1)} %get-tuple-element.185, f32[2,12,10,130]{1,3,2,0:T(8,128)S(1)} %scatter.31, f32[8,128]{1,0:T(8,128)S(1)} %get-tuple-element.189, f32[8,128]{1,0:T(8,128)S(1)} %get-tuple-element.188, ...), kind=kLoop, calls=%fused_computation.62 | loop fusion | flops 270336 | bytes 905216 | tf_op jit(solution)/shard_map/div | solution.py:156
  24.4 0.3 copy.214
  24.7 0.3 copy.215
  25.4 1.7 %collective-permute-start.5 = (f32[72,1,128]{2,1,0:T(1,128)S(1)}, f32[72,1,128]{2,1,0:T(1,128)S(1)}, u32[]{:S(2)}, u32[]{:S(2)}) collective-permute-start(f32[72,1,128]{2,1,0:T(1,128)S(1)} %get-tuple-element.209), channel_id=1, source_target_pairs={{8,0},{16,8},{24,16},{0,24},{9,1},{17,9},{25,17},{1,25},{10,2},{18... | collective-permute-start | bytes 110600 | tf_op jit(solution)/shard_map/ppermute | solution.py:21
  27.2 0.6 fusion.47
  27.8 1.0 collective-permute-done.4
  28.9 1.1 fusion.67
  30.0 1.3 %copy.216 = f32[72,10,1]{0,2,1:T(1,128)S(1)} copy(f32[72,10,1]{2,1,0:T(8,128)} %get-tuple-element.206) | data formatting | bytes 5760 | tf_op jit(solution)/shard_map/slice | solution.py:16
  31.8 4.5 %collective-permute-start.7 = (f32[72,10,1]{0,2,1:T(1,128)S(1)}, f32[72,10,1]{0,2,1:T(1,128)S(1)}, u32[]{:S(2)}, u32[]{:S(2)}) collective-permute-start(f32[72,10,1]{0,2,1:T(1,128)S(1)} %copy.217), channel_id=1, source_target_pairs={{1,0},{2,1},{3,2},{4,3},{5,4},{6,5},{7,6},{0,7},{9,8},{10,9},{11,1... | collective-permute-start | bytes 8648 | tf_op jit(solution)/shard_map/ppermute | solution.py:21
  36.2 1.4 %copy.213 = f32[2,12,8,128]{1,3,2,0:T(8,128)} copy(f32[2,12,8,128]{3,2,1,0:T(8,128)S(1)} %copy-done.5) | data formatting | bytes 196608 | tf_op args[1]
  37.6 0.3 copy.218
  38.0 1.1 copy.219
  39.1 3.0 %pad_maximum_fusion = f32[72,10,130]{2,1,0:T(8,128)} fusion(f32[72,10,1]{2,1,0:T(8,128)} %copy.219, f32[72,1,128]{2,1,0:T(1,128)S(1)} %collective-permute-done.5, f32[72,8,128]{2,1,0:T(8,128)S(1)} %bitcast.123, f32[72,1,128]{2,1,0:T(1,128)S(1)} %collective-permute-done.4, f32[72,10,1]{2,1,0:T(8,128)S(1)} %copy.218), kind=kLoop, calls=%fused_computation.7 | loop fusion | flops 374400 | bytes 748800 | tf_op jit(solution)/shard_map/concatenate | solution.py:17
  42.0 1.8 %copy.223 = f32[2,36,10,130]{1,3,2,0:T(8,128)S(1)} copy(f32[2,36,10,130]{3,2,1,0:T(8,128)} %bitcast.119) | data formatting | bytes 748800 | tf_op jit(solution)/shard_map/reshape | solution.py:162
  44.4 1.8 %fusion.10 = f32[2,36,8,128]{1,3,2,0:T(8,128)S(1)} fusion(f32[2,36,10,130]{1,3,2,0:T(8,128)S(1)} %scatter.39, f32[8,128]{1,0:T(8,128)} %copy-done.8, f32[8,128]{1,0:T(8,128)} %copy-done.7, f32[8,128]{1,0:T(8,128)S(1)} %get-tuple-element.187, f32[8,128]{1,0:T(8,128)S(1)} %get-tuple-element.186, f32[8,128]{1,0:T(8,128)S(1)} %get-tuple-element.185), kind=kLoop, calls=%fused_computation.28 | loop fusion | flops 663552 | bytes 1789952 | tf_op jit(solution)/shard_map/sub | solution.py:59
  46.2 1.1 pad_maximum_fusion.1
  47.4 1.1 convolution_bitcast_fusion.2
  48.5 1.0 convolution_bitcast_fusion.4
  49.5 1.1 fusion.5
  50.7 1.0 fusion.6
  51.7 1.8 %convolution_bitcast_fusion.5 = f32[48,48]{1,0:T(8,128)S(1)} fusion(f32[2,48,1024]{1,2,0:T(8,128)S(1)} %bitcast.117), kind=kOutput, calls=%fused_computation.18 | convolution fusion | flops 56623104 | bytes 402432 | tf_op jit(solution)/shard_map/pjc,pkc->jk/dot_general | solution.py:66
  53.5 1.8 %convolution_bitcast_fusion.6 = f32[48,48]{1,0:T(8,128)S(1)} fusion(f32[2,48,1024]{1,2,0:T(8,128)S(1)} %bitcast.118, f32[2,48,1024]{1,2,0:T(8,128)S(1)} %bitcast.120), kind=kOutput, calls=%fused_computation.19 | convolution fusion | flops 56623104 | bytes 795648 | tf_op jit(solution)/shard_map/pjc,pkc->jk/dot_general | solution.py:66
  55.3 38.7 %all-reduce.2 = (f32[48,48]{1,0:T(8,128)S(1)}, f32[48,48]{1,0:T(8,128)S(1)}, f32[48,48]{1,0:T(8,128)S(1)}, f32[48,48]{1,0:T(8,128)S(1)}) all-reduce(f32[48,48]{1,0:T(8,128)S(1)} %convolution_bitcast_fusion.5, f32[48,48]{1,0:T(8,128)S(1)} %convolution_bitcast_fusion.6, ...), channel_id=1, replica_groups=mesh['row'=4,'col'=8] {'col'}, use_global_device_ids=true, to_apply=%region_3.4 | all-reduce | flops 9216 | bytes 73728 | tf_op jit(solution)/shard_map/psum | solution.py:172
  94.0 11.3 %all-reduce.3 = (f32[48,48]{1,0:T(8,128)S(1)}, f32[48,48]{1,0:T(8,128)S(1)}, f32[48,48]{1,0:T(8,128)S(1)}, f32[48,48]{1,0:T(8,128)S(1)}) all-reduce(f32[48,48]{1,0:T(8,128)S(1)} %get-tuple-element.175, f32[48,48]{1,0:T(8,128)S(1)} %get-tuple-element.176, ...), channel_id=1, replica_groups=mesh['row'=4,'col'=8] {'row'}, use_global_device_ids=true, to_apply=%region_4.5 | all-reduce | flops 9216 | bytes 73728 | tf_op jit(solution)/shard_map/psum | solution.py:171
  105.3 1.0 gather_fusion
  106.3 1.0 gather_fusion.1
  108.9 0.7 multiply_reduce_fusion
  110.8 3.7 %while.21 = (s32[]{:T(128)}, f32[72,72]{0,1:T(8,128)S(1)}, f32[72,72]{1,0:T(8,128)S(1)}, s32[]{:T(128)}) while((s32[]{:T(128)}, f32[72,72]{0,1:T(8,128)S(1)}, f32[72,72]{1,0:T(8,128)S(1)}, s32[]{:T(128)}) %tuple.94), condition=%wide.region_9.10_spmd.clone, body=%wide.region_8.9_spmd.clone.sunk | while | flops 13457666 | bytes 269621 | solution.py:90
  115.1 1.1 copy-done.1
  116.5 0.6 pad_maximum_fusion.2
  117.1 0.6 fusion.24
  117.8 0.7 fusion.23
  120.3 0.6 copy.245
  120.9 0.7 fusion.4
  121.6 0.6 fusion.3
  122.3 0.8 copy.244
  (111 shorter events, 10.6 us)
Async XLA Ops:
  0.6 13.7 %copy-start.6 = (f32[2,12,8,128]{3,2,1,0:T(8,128)S(1)}, f32[2,12,8,128]{3,2,1,0:T(8,128)}, u32[]{:S(2)}) copy-start(f32[2,12,8,128]{3,2,1,0:T(8,128)} %param.23) | copy-start | bytes 294916
  3.1 4.7 %collective-permute-start = (f32[25,1,128]{2,0,1:T(8,128)S(1)}, f32[25,1,128]{2,0,1:T(8,128)S(1)}, u32[]{:S(2)}, u32[]{:S(2)}) collective-permute-start(f32[25,1,128]{2,0,1:T(8,128)S(1)} %get-tuple-element.212), channel_id=1, source_target_pairs={{0,8},{8,16},{16,24},{24,0},{1,9},{9,17},{17,25},{25,1},{2,10},{10... | collective-permute-start | bytes 38408 | tf_op jit(solution)/shard_map/ppermute | solution.py:19
  3.6 4.2 %collective-permute-start.1 = (f32[25,1,128]{2,0,1:T(8,128)S(1)}, f32[25,1,128]{2,0,1:T(8,128)S(1)}, u32[]{:S(2)}, u32[]{:S(2)}) collective-permute-start(f32[25,1,128]{2,0,1:T(8,128)S(1)} %get-tuple-element.213), channel_id=1, source_target_pairs={{8,0},{16,8},{24,16},{0,24},{9,1},{17,9},{25,17},{1,25},{10,2},{18... | collective-permute-start | bytes 38408 | tf_op jit(solution)/shard_map/ppermute | solution.py:21
  7.9 10.3 %collective-permute-start.2 = (f32[25,10,1]{2,0,1:T(8,128)S(1)}, f32[25,10,1]{2,0,1:T(8,128)S(1)}, u32[]{:S(2)}, u32[]{:S(2)}) collective-permute-start(f32[25,10,1]{2,0,1:T(8,128)S(1)} %get-tuple-element.210), channel_id=1, source_target_pairs={{0,1},{1,2},{2,3},{3,4},{4,5},{5,6},{6,7},{7,0},{8,9},{9,10},{10,1... | collective-permute-start | bytes 3008 | tf_op jit(solution)/shard_map/ppermute | solution.py:19
  10.2 10.1 %collective-permute-start.3 = (f32[25,10,1]{2,0,1:T(8,128)S(1)}, f32[25,10,1]{2,0,1:T(8,128)S(1)}, u32[]{:S(2)}, u32[]{:S(2)}) collective-permute-start(f32[25,10,1]{2,0,1:T(8,128)S(1)} %get-tuple-element.211), channel_id=1, source_target_pairs={{1,0},{2,1},{3,2},{4,3},{5,4},{6,5},{7,6},{0,7},{9,8},{10,9},{11,1... | collective-permute-start | bytes 3008 | tf_op jit(solution)/shard_map/ppermute | solution.py:21
  21.5 2.9 %copy-start.7 = (f32[8,128]{1,0:T(8,128)}, f32[8,128]{1,0:T(8,128)S(1)}, u32[]{:S(2)}) copy-start(f32[8,128]{1,0:T(8,128)S(1)} %get-tuple-element.188) | copy-start | bytes 12292
  21.5 2.9 %copy-start.8 = (f32[8,128]{1,0:T(8,128)}, f32[8,128]{1,0:T(8,128)S(1)}, u32[]{:S(2)}) copy-start(f32[8,128]{1,0:T(8,128)S(1)} %get-tuple-element.189) | copy-start | bytes 12292
  24.4 0.9 copy-start.5
  25.4 3.4 %collective-permute-start.4 = (f32[72,1,128]{2,1,0:T(1,128)S(1)}, f32[72,1,128]{2,1,0:T(1,128)S(1)}, u32[]{:S(2)}, u32[]{:S(2)}) collective-permute-start(f32[72,1,128]{2,1,0:T(1,128)S(1)} %get-tuple-element.208), channel_id=1, source_target_pairs={{0,8},{8,16},{16,24},{24,0},{1,9},{9,17},{17,25},{25,1},{2,10},{10... | collective-permute-start | bytes 110600 | tf_op jit(solution)/shard_map/ppermute | solution.py:19
  25.4 3.4 %collective-permute-start.5 = (f32[72,1,128]{2,1,0:T(1,128)S(1)}, f32[72,1,128]{2,1,0:T(1,128)S(1)}, u32[]{:S(2)}, u32[]{:S(2)}) collective-permute-start(f32[72,1,128]{2,1,0:T(1,128)S(1)} %get-tuple-element.209), channel_id=1, source_target_pairs={{8,0},{16,8},{24,16},{0,24},{9,1},{17,9},{25,17},{1,25},{10,2},{18... | collective-permute-start | bytes 110600 | tf_op jit(solution)/shard_map/ppermute | solution.py:21
  31.2 6.4 %collective-permute-start.6 = (f32[72,10,1]{0,2,1:T(1,128)S(1)}, f32[72,10,1]{0,2,1:T(1,128)S(1)}, u32[]{:S(2)}, u32[]{:S(2)}) collective-permute-start(f32[72,10,1]{0,2,1:T(1,128)S(1)} %copy.216), channel_id=1, source_target_pairs={{0,1},{1,2},{2,3},{3,4},{4,5},{5,6},{6,7},{7,0},{8,9},{9,10},{10,1... | collective-permute-start | bytes 8648 | tf_op jit(solution)/shard_map/ppermute | solution.py:19
  31.8 6.2 %collective-permute-start.7 = (f32[72,10,1]{0,2,1:T(1,128)S(1)}, f32[72,10,1]{0,2,1:T(1,128)S(1)}, u32[]{:S(2)}, u32[]{:S(2)}) collective-permute-start(f32[72,10,1]{0,2,1:T(1,128)S(1)} %copy.217), channel_id=1, source_target_pairs={{1,0},{2,1},{3,2},{4,3},{5,4},{6,5},{7,6},{0,7},{9,8},{10,9},{11,1... | collective-permute-start | bytes 8648 | tf_op jit(solution)/shard_map/ppermute | solution.py:21
  44.4 1.8 %copy-start = (f32[2,12,8,128]{1,3,2,0:T(8,128)S(1)}, f32[2,12,8,128]{1,3,2,0:T(8,128)}, u32[]{:S(2)}) copy-start(f32[2,12,8,128]{1,3,2,0:T(8,128)} %copy.212) | copy-start | bytes 294916
  44.4 1.8 %copy-start.2 = (f32[2,12,8,128]{1,3,2,0:T(8,128)S(1)}, f32[2,12,8,128]{1,3,2,0:T(8,128)}, u32[]{:S(2)}) copy-start(f32[2,12,8,128]{1,3,2,0:T(8,128)} %get-tuple-element.184) | copy-start | bytes 294916
  44.4 1.9 %copy-start.3 = (f32[2,12,8,128]{1,3,2,0:T(8,128)S(1)}, f32[2,12,8,128]{1,3,2,0:T(8,128)}, u32[]{:S(2)}) copy-start(f32[2,12,8,128]{1,3,2,0:T(8,128)} %copy.213) | copy-start | bytes 294916
  53.5 53.8 %copy-start.9 = (f32[12,12]{1,0:T(8,128)S(1)}, f32[12,12]{1,0:T(8,128)}, u32[]{:S(2)}) copy-start(f32[12,12]{1,0:T(8,128)} %fusion.47) | copy-start | bytes 1732
  115.0 1.2 copy-start.1
  115.0 1.5 %copy-start.4 = (f32[2,12,8,128]{1,3,2,0:T(8,128)S(1)}, f32[2,12,8,128]{1,3,2,0:T(8,128)}, u32[]{:S(2)}) copy-start(f32[2,12,8,128]{1,3,2,0:T(8,128)} %copy.213) | copy-start | bytes 294916
